TPU v7x, 256 devices: a whole 4x4x8 slice. The times are simulated.
256 devices in a mesh: lat: 8 (over y, z_lo), lon: 8 (over x, core), dp: 4 (over z_hi).
Axes of the slice: x: 4, y: 4, z: 8 (z_hi: 4, z_lo: 2; z = z_hi * 2 + z_lo), core: 2. Of those that a mesh axis runs over, the one named last changes fastest.
Arguments:
- state_grid: bfloat16 [4, 384, 768, 128], P('dp', ('lat', 'lon')), may hold values from -6 to 6
- cotangent: bfloat16 [4, 384, 768, 128], P('dp', ('lat', 'lon')), may hold values from -6 to 6
- legendre: bfloat16 [384, 384, 384], P(('lat', 'lon')), may hold values from -0.3125 to 0.3125
- wave_ids: int32 [384], replicated, may hold values from 0 to 383, each once
- weights: bfloat16 [384, 2, 4, 1024], P('lat'), may hold values from -0.75 to 0.75
Outputs:
- input_grad: bfloat16 [4, 384, 768, 128], P('dp', ('lat', 'lon'))
- weight_grad: float32 [384, 2, 4, 1024], P('lat')
Inputs may be any that keep to these rules, and one draw needn't show every extreme that they name: wave_ids[j] is the wavenumber of slot j; each of 0 to 383 stands in exactly one slot.
All inputs are finite; a program needn't handle non-finite values.
Results may differ from a plain program's by a relative error of at most 0.034.
Values may be sent and summed in bfloat16 or wider, within the bound.
No kernel may reach another device: no remote copies, remote signals or barrier semaphores. Data moves between devices by JAX's collectives and lax.ppermute only.
A program may use at most 128 MiB of HBM per device.

v0:
```python
import math
import jax
import jax.numpy as jnp
from jax import lax
from jax.sharding import PartitionSpec as P

NLON = 768
GROUPS = 4
GROUP_WIDTH = 32


def build_tables(wave_ids):
    columns = jnp.arange(NLON, dtype=jnp.int32)
    phase_int = wave_ids[:, None] * columns[None, :] % NLON
    angles = phase_int.astype(jnp.float32) * jnp.float32(2.0 * math.pi / NLON)
    factor = jnp.float32(1.0 / math.sqrt(NLON))
    paired = jnp.stack([jnp.cos(angles) * factor, -jnp.sin(angles) * factor], axis=1)
    forward_table = paired.reshape(2 * wave_ids.shape[0], NLON)
    doubling = jnp.where(wave_ids == 0, 1.0, 2.0).astype(jnp.float32)
    inverse_table = forward_table * jnp.repeat(doubling, 2)[:, None]
    return (forward_table.astype(jnp.bfloat16), inverse_table.astype(jnp.bfloat16))


def build_kernel(weights):
    degree_count = weights.shape[0]
    real_part = weights[:, 0].reshape(degree_count, GROUPS, GROUP_WIDTH, GROUP_WIDTH)
    imag_part = weights[:, 1].reshape(degree_count, GROUPS, GROUP_WIDTH, GROUP_WIDTH)
    upper_rows = jnp.stack([real_part, imag_part], axis=3)
    lower_rows = jnp.stack([-imag_part, real_part], axis=3)
    return jnp.stack([upper_rows, lower_rows], axis=2)


def gelu_slope(branch):
    normal_cdf = 0.5 * (1.0 + lax.erf(branch * (1.0 / math.sqrt(2.0))))
    density = jnp.exp(-0.5 * branch * branch) * (1.0 / math.sqrt(2.0 * math.pi))
    return normal_cdf + branch * density


def shards(state_grid, cotangent, legendre, wave_ids, weights):
    lat_count = lax.axis_size("lat")
    lon_count = lax.axis_size("lon")
    samples, rows_dev, lon_cells, channels = state_grid.shape
    slot_count, lat_cells, degree_count = legendre.shape
    slot_reals = 2 * slot_count
    first_slot = (lax.axis_index("lat") * lon_count + lax.axis_index("lon")) * slot_count
    held_waves = lax.dynamic_slice_in_dim(wave_ids, first_slot, slot_count)
    degree_ids = jnp.arange(degree_count, dtype=jnp.int32)
    masked = jnp.where(
        degree_ids[None, None, :] >= held_waves[:, None, None],
        legendre,
        jnp.zeros((), legendre.dtype),
    )
    slot_order = wave_ids.reshape(lat_count, lon_count, slot_count).transpose(1, 0, 2).reshape(-1)
    forward_table, inverse_table = build_tables(slot_order)
    kernel = build_kernel(weights)

    def analyze(source, twiddle):
        spectra = jnp.einsum(
            "srnc,kn->srkc", source, twiddle, preferred_element_type=jnp.float32
        ).astype(jnp.bfloat16)
        gathered = lax.all_to_all(
            lax.all_to_all(spectra, "lon", split_axis=2, concat_axis=1, tiled=True),
            "lat",
            split_axis=2,
            concat_axis=1,
            tiled=True,
        )
        blocks = gathered.reshape(samples, lat_cells, slot_count, 2 * channels)
        spectral = jnp.einsum("samc,mal->slmc", blocks, masked, preferred_element_type=jnp.float32)
        spectral = spectral.astype(jnp.bfloat16).reshape(
            samples, degree_count, slot_reals, channels
        )
        return lax.all_to_all(spectral, "lat", split_axis=1, concat_axis=2, tiled=True)

    def synthesize(spectral, twiddle):
        joined = lax.all_to_all(spectral, "lat", split_axis=2, concat_axis=1, tiled=True)
        blocks = joined.reshape(samples, degree_count, slot_count, 2 * channels)
        spectra = jnp.einsum(
            "slmc,mal->samc", blocks, masked, preferred_element_type=jnp.float32
        ).astype(jnp.bfloat16)
        spectra = spectra.reshape(samples, lat_cells, slot_reals, channels)
        pencil = lax.all_to_all(
            lax.all_to_all(spectra, "lat", split_axis=1, concat_axis=2, tiled=True),
            "lon",
            split_axis=1,
            concat_axis=2,
            tiled=True,
        )
        return jnp.einsum("srkc,kn->srnc", pencil, twiddle, preferred_element_type=jnp.float32)

    def split_groups(spectral):
        return spectral.reshape(samples, spectral.shape[1], -1, 2, GROUPS, GROUP_WIDTH)

    coef_fwd = analyze(state_grid, forward_table)
    coef_six = split_groups(coef_fwd)
    mixed_coef = jnp.einsum(
        "slmpgi,lgpiqo->slmqgo", coef_six, kernel, preferred_element_type=jnp.float32
    ).astype(jnp.bfloat16)
    branch = synthesize(mixed_coef.reshape(coef_fwd.shape), inverse_table)
    pulled = (cotangent.astype(jnp.float32) * gelu_slope(branch)).astype(jnp.bfloat16)
    back_coef = analyze(pulled, inverse_table)
    back_six = split_groups(back_coef)
    outer_sums = jnp.einsum(
        "slmpgi,slmqgo->lgpiqo", coef_six, back_six, preferred_element_type=jnp.float32
    )
    real_grad = outer_sums[:, :, 0, :, 0, :] + outer_sums[:, :, 1, :, 1, :]
    imag_grad = outer_sums[:, :, 0, :, 1, :] - outer_sums[:, :, 1, :, 0, :]
    local_grad = jnp.stack([real_grad, imag_grad], axis=1).reshape(weights.shape)
    weight_grad = lax.psum(local_grad.astype(jnp.bfloat16), ("lon", "dp")).astype(jnp.float32)
    demixed = jnp.einsum(
        "slmqgo,lgpiqo->slmpgi", back_six, kernel, preferred_element_type=jnp.float32
    ).astype(jnp.bfloat16)
    returned = synthesize(demixed.reshape(back_coef.shape), forward_table)
    input_grad = (cotangent.astype(jnp.float32) + returned).astype(jnp.bfloat16)
    return (input_grad, weight_grad)


def solution(mesh):
    return jax.shard_map(
        shards,
        mesh=mesh,
        in_specs=(
            P("dp", ("lat", "lon"), None, None),
            P("dp", ("lat", "lon"), None, None),
            P(("lat", "lon"), None, None),
            P(),
            P("lat", None, None, None),
        ),
        out_specs=(P("dp", ("lat", "lon"), None, None), P("lat", None, None, None)),
        check_vma=False,
    )
```

profile of v0, /device:TPU:8, one launch (start us, length us, event | category | flops | bytes accessed | tf_op | source)
XLA Modules:
  0.0 725.3 jit_solution(13457028617643623277)
XLA Ops:
  8.2 4.9 cosine_multiply_fusion
  13.3 2.2 copy.215
  15.6 3.7 reshape.366
  19.3 2.4 fusion.14
  22.5 25.9 %all_to_all.192 = bf16[1,6,768,128]{3,1,0,2:T(8,128)(2,1)S(1)} all-to-all(bf16[1,6,768,128]{3,1,0,2:T(8,128)(2,1)S(1)} %copy.223), channel_id=1, replica_groups=mesh['lat'=8,'lon'=8,'dp'=4] {'lon'}, dimensions={2} | all-to-all | bytes 2359296 | tf_op jit(solution)/shard_map/all_to_all | solution.py:62
  48.7 1.5 copy.226
  50.1 6.5 all-to-all-start.1
  57.4 13.8 %all-to-all-done.1 = bf16[1,48,96,128]{3,1,0,2:T(8,128)(2,1)S(1)} async-done(((bf16[1,48,96,128]{3,1,0,2:T(8,128)(2,1)}), bf16[1,48,96,128]{3,1,0,2:T(8,128)(2,1)S(1)}, u32[]{:S(2)}, u32[]{:S(2)}) %all-to-all-start.1) | async-done | bytes 1179680 | tf_op jit(solution)/shard_map/all_to_all | solution.py:61
  71.2 3.0 copy.280
  74.2 4.4 reshape.378
  78.7 3.4 convolution_convert_fusion.1
  82.1 2.9 copy.229
  85.0 6.4 all-to-all-start.2
  92.5 1.6 copy.298
  95.3 2.2 copy.299
  97.5 2.7 maximum_bitcast_fusion
  100.2 3.0 pad_maximum_fusion
  103.2 12.7 %copy.232 = bf16[48,4,2,32,2,32]{3,5,2,4,1,0:T(8,128)(2,1)} copy(bf16[48,4,2,32,2,32]{0,5,4,3,1,2:T(8,128)(2,1)} %pad_maximum_fusion) | data formatting | bytes 3145728 | tf_op jit(solution)/shard_map/stack | solution.py:30
  115.8 1.7 copy.230
  117.6 2.7 copy.231
  120.3 8.3 %copy.270 = bf16[48,48,2,4,32,1]{1,4,2,5,3,0:T(8,128)(2,1)} copy(bf16[48,48,2,4,32,1]{0,4,3,2,1,5:T(8,128)(2,1)} %bitcast.179) | data formatting | bytes 2359296 | tf_op jit(solution)/shard_map/reshape.8
  128.5 6.7 fusion
  135.3 8.3 %copy.234 = bf16[1,48,48,2,4,32]{1,5,4,3,2,0:T(8,128)(2,1)} copy(bf16[1,48,48,2,4,32]{2,5,3,4,1,0:T(8,128)(2,1)} %fusion) | data formatting | bytes 2359296 | tf_op jit(solution)/shard_map/convert_element_type | solution.py:98
  143.5 3.2 copy.235
  146.7 19.4 %all_to_all.193 = bf16[1,48,96,128]{3,1,0,2:T(8,128)(2,1)} all-to-all(bf16[1,48,96,128]{3,1,0,2:T(8,128)(2,1)S(1)} %copy.235), channel_id=1, replica_groups=mesh['lat'=8,'lon'=8,'dp'=4] {'lat'}, dimensions={2} | all-to-all | bytes 2359296 | tf_op jit(solution)/shard_map/all_to_all | solution.py:76
  166.2 4.2 copy.283
  170.4 4.4 reshape.379
  174.8 3.5 convolution_convert_fusion.3
  178.3 2.9 copy.238
  181.2 21.5 %all_to_all.194 = bf16[1,384,12,128]{3,2,0,1:T(8,128)(2,1)S(1)} all-to-all(bf16[1,384,12,128]{3,2,0,1:T(8,128)(2,1)} %copy.238), channel_id=1, replica_groups=mesh['lat'=8,'lon'=8,'dp'=4] {'lat'}, dimensions={1} | all-to-all | bytes 2359296 | tf_op jit(solution)/shard_map/all_to_all | solution.py:83
  204.4 4.3 all-to-all-start.5
  211.1 14.9 %all-to-all-done.5 = bf16[1,48,96,128]{3,2,0,1:T(8,128)(2,1)} async-done(((bf16[1,48,96,128]{3,2,0,1:T(8,128)(2,1)}), bf16[1,48,96,128]{3,2,0,1:T(8,128)(2,1)}, u32[]{:S(2)}, u32[]{:S(2)}) %all-to-all-start.5) | async-done | bytes 1179680 | tf_op jit(solution)/shard_map/all_to_all | solution.py:82
  227.4 4.8 fusion.15
  232.3 2.1 copy.244
  234.4 24.2 %all_to_all.195 = bf16[1,6,768,128]{3,1,0,2:T(8,128)(2,1)S(1)} all-to-all(bf16[1,6,768,128]{3,1,0,2:T(8,128)(2,1)S(1)} %copy.244), channel_id=1, replica_groups=mesh['lat'=8,'lon'=8,'dp'=4] {'lon'}, dimensions={2} | all-to-all | bytes 2359296 | tf_op jit(solution)/shard_map/all_to_all | solution.py:62
  259.3 20.1 %all_to_all.196 = bf16[1,48,96,128]{3,1,0,2:T(8,128)(2,1)S(1)} all-to-all(bf16[1,48,96,128]{3,1,0,2:T(8,128)(2,1)S(1)} %copy.247), channel_id=1, replica_groups=mesh['lat'=8,'lon'=8,'dp'=4] {'lat'}, dimensions={2} | all-to-all | bytes 2359296 | tf_op jit(solution)/shard_map/all_to_all | solution.py:61
  279.4 3.0 copy.284
  282.4 4.4 reshape.380
  286.8 2.4 convolution_convert_fusion
  289.2 2.0 copy.250
  291.1 5.1 all-to-all-start.8
  296.3 11.6 %copy.253 = bf16[48,4,2,32,2,32]{5,3,4,2,1,0:T(8,128)(2,1)} copy(bf16[48,4,2,32,2,32]{0,5,4,3,1,2:T(8,128)(2,1)} %pad_maximum_fusion) | data formatting | bytes 3145728 | tf_op jit(solution)/shard_map/stack | solution.py:30
  307.8 6.3 all-to-all-done.8
  314.5 2.7 copy.252
  317.2 8.3 %copy.273 = bf16[48,48,2,4,32,1]{1,4,2,5,3,0:T(8,128)(2,1)} copy(bf16[48,48,2,4,32,1]{0,4,3,2,1,5:T(8,128)(2,1)} %bitcast.182) | data formatting | bytes 2359296 | tf_op jit(solution)/shard_map/reshape.39
  325.5 6.8 fusion.1
  332.3 8.3 %copy.255 = bf16[1,48,48,2,4,32]{1,5,4,3,2,0:T(8,128)(2,1)} copy(bf16[1,48,48,2,4,32]{2,5,3,4,1,0:T(8,128)(2,1)} %fusion.1) | data formatting | bytes 2359296 | tf_op jit(solution)/shard_map/convert_element_type | solution.py:112
  340.6 3.2 copy.256
  343.8 19.7 %all_to_all.197 = bf16[1,48,96,128]{3,1,0,2:T(8,128)(2,1)S(1)} all-to-all(bf16[1,48,96,128]{3,1,0,2:T(8,128)(2,1)S(1)} %copy.256), channel_id=1, replica_groups=mesh['lat'=8,'lon'=8,'dp'=4] {'lat'}, dimensions={2} | all-to-all | bytes 2359296 | tf_op jit(solution)/shard_map/all_to_all | solution.py:76
  363.5 3.0 copy.287
  366.4 4.4 reshape.381
  370.9 2.4 convolution_convert_fusion.2
  373.3 2.0 copy.259
  375.3 5.3 all-to-all-start.10
  380.6 8.3 %copy.276 = bf16[48,48,2,4,32,1]{1,4,5,2,3,0:T(8,128)(2,1)} copy(bf16[48,48,2,4,32,1]{0,4,3,2,1,5:T(8,128)(2,1)} %bitcast.180) | data formatting | bytes 2359296 | tf_op jit(solution)/shard_map/reshape.8
  388.9 12.5 %fusion.41 = f32[48,4,2,32,2,32]{5,3,4,2,1,0:T(8,128)} fusion(bf16[48,48,2,4,32,1]{1,4,5,2,3,0:T(8,128)(2,1)} %copy.276, bf16[48,48,2,4,32,1]{1,4,2,5,3,0:T(8,128)(2,1)} %copy.273), kind=kOutput, calls=%fused_computation.66 | convolution fusion | flops 75497472 | bytes 5505024 | tf_op jit(solution)/shard_map/slmpgi,slmqgo->lgpiqo/dot_general | solution.py:103
  403.1 4.3 all-to-all-start.11
  407.4 7.5 %fusion.3 = (bf16[48,4,1,32,1,32]{5,3,4,2,1,0:T(8,128)(2,1)}, bf16[48,4,1,32,1,32]{5,3,4,2,1,0:T(8,128)(2,1)S(1)}) fusion(f32[48,4,2,32,2,32]{5,3,4,2,1,0:T(8,128)} %fusion.41), kind=kLoop, calls=%fused_computation.9 | loop fusion | flops 786432 | bytes 3932160 | tf_op jit(solution)/shard_map/convert.3
  415.0 2.9 reshape.382
  418.0 1.5 reshape.383
  421.6 290.0 %all-reduce.2.cloned.1.call-done = bf16[48,2,4,1024]{3,0,2,1:T(8,128)(2,1)} async-done(((bf16[48,2,4,1024]{3,0,2,1:T(8,128)(2,1)}), bf16[48,2,4,1024]{3,0,2,1:T(8,128)(2,1)}) %all-reduce.2.cloned.1.call-update) | async-done | bytes 786448 | tf_op jit(solution)/shard_map/psum | solution.py:109
  711.6 2.9 copy.269
  714.5 1.5 copy.263
  716.1 2.1 fusion.5
  (46 shorter events, 16.0 us)
Async XLA Ops:
  7.2 12.2 %copy-start = (bf16[1,6,768,128]{3,2,1,0:T(8,128)(2,1)S(1)}, bf16[1,6,768,128]{3,2,1,0:T(8,128)(2,1)}, u32[]{:S(2)}) copy-start(bf16[1,6,768,128]{3,2,1,0:T(8,128)(2,1)} %param.5) | copy-start | bytes 3538948
  50.1 21.1 %all-to-all-start.1 = ((bf16[1,48,96,128]{3,1,0,2:T(8,128)(2,1)}), bf16[1,48,96,128]{3,1,0,2:T(8,128)(2,1)S(1)}, u32[]{:S(2)}, u32[]{:S(2)}) async-start(bf16[1,48,96,128]{3,1,0,2:T(8,128)(2,1)} %copy.226), calls=%async_computation.1 | async-start | bytes 2359296 | tf_op jit(solution)/shard_map/all_to_all | solution.py:61
  85.0 6.4 copy-start.3
  85.0 30.9 %all-to-all-start.2 = ((bf16[1,384,12,128]{3,2,0,1:T(8,128)(2,1)}), bf16[1,384,12,128]{3,2,0,1:T(8,128)(2,1)}, u32[]{:S(2)}, u32[]{:S(2)}) async-start(bf16[1,384,12,128]{3,2,0,1:T(8,128)(2,1)} %copy.229), calls=%async_computation.2 | async-start | bytes 3145728 | tf_op jit(solution)/shard_map/all_to_all | solution.py:73
  204.4 21.6 %all-to-all-start.5 = ((bf16[1,48,96,128]{3,2,0,1:T(8,128)(2,1)}), bf16[1,48,96,128]{3,2,0,1:T(8,128)(2,1)}, u32[]{:S(2)}, u32[]{:S(2)}) async-start(bf16[1,48,96,128]{3,2,0,1:T(8,128)(2,1)} %copy.241), calls=%async_computation.5 | async-start | bytes 2359296 | tf_op jit(solution)/shard_map/all_to_all | solution.py:82
  291.1 23.0 %all-to-all-start.8 = ((bf16[1,384,12,128]{3,2,0,1:T(8,128)(2,1)}), bf16[1,384,12,128]{3,2,0,1:T(8,128)(2,1)S(1)}, u32[]{:S(2)}, u32[]{:S(2)}) async-start(bf16[1,384,12,128]{3,2,0,1:T(8,128)(2,1)} %copy.250), calls=%async_computation.8 | async-start | bytes 3145728 | tf_op jit(solution)/shard_map/all_to_all | solution.py:73
  375.3 26.1 %all-to-all-start.10 = ((bf16[1,384,12,128]{3,2,0,1:T(8,128)(2,1)}), bf16[1,384,12,128]{3,2,0,1:T(8,128)(2,1)S(1)}, u32[]{:S(2)}, u32[]{:S(2)}) async-start(bf16[1,384,12,128]{3,2,0,1:T(8,128)(2,1)} %copy.259), calls=%async_computation.10 | async-start | bytes 3145728 | tf_op jit(solution)/shard_map/all_to_all | solution.py:83
  403.1 311.3 %all-to-all-start.11 = ((bf16[1,48,96,128]{3,2,0,1:T(8,128)(2,1)}), bf16[1,48,96,128]{3,2,0,1:T(8,128)(2,1)}, u32[]{:S(2)}, u32[]{:S(2)}) async-start(bf16[1,48,96,128]{3,2,0,1:T(8,128)(2,1)} %copy.262), calls=%async_computation.11 | async-start | bytes 2359296 | tf_op jit(solution)/shard_map/all_to_all | solution.py:82
  407.4 304.2 %all-reduce.2.cloned.1.call-start = ((), (), s32[]{:S(2)}) async-start(), calls=%async_computation.12 | async-start | bytes 1572864 | tf_op jit(solution)/shard_map/psum | solution.py:109
  419.5 1.6 copy-start.2
  714.5 1.6 copy-start.4
  716.1 2.1 copy-start.1
Sparse Core Ops, SparseCore 0:
  420.8 290.7 all-reduce.1
where the time goes:
time: 735 us; the launch traced here: 725 us
  waiting for transfers between devices  325 us (44%)
  local copies, waits for them, and re-layouts  155 us (21%)
  blocking collectives  131 us (18%)
  matrix products  47 us (6%)
  starting transfers between devices  31.8 us (4%)
  other arithmetic  20.7 us (3%)
  between operations  14.6 us (2%)
    psum x1, waiting for transfers between devices, shards(): lax.psum(local_grad.astype(jnp.bfloat16), ('lon', 'dp')).astype(jnp.float32)  290 us
    another operation x11, local copies, waits for them, and re-layouts  55.7 us
    all_to_all x2, blocking collectives, analyze(): lax.all_to_all(spectra, 'lon', split_axis=2, concat_axis=1, tiled=True)  50.1 us
    all_to_all x2, blocking collectives, synthesize(): lax.all_to_all(spectral, 'lat', split_axis=2, concat_axis=1, tiled=True)  39.1 us
    another operation x2, local copies, waits for them, and re-layouts, build_kernel(): return jnp.stack([upper_rows, lower_rows], axis=2)  24.2 us
    all_to_all x1, blocking collectives, synthesize(): lax.all_to_all(spectra, 'lat', split_axis=1, concat_axis=2, tiled=True)  21.5 us
    all_to_all x1, blocking collectives, analyze(): lax.all_to_all(lax.all_to_all(spectra, 'lon', split_axis=2, concat_axis=1...  20.1 us
    all_to_all x2, waiting for transfers between devices, synthesize(): lax.all_to_all(lax.all_to_all(spectra, 'lat', split_axis=1, concat_axis=2...  14.9 us
  transfers between devices with their start and end apart: 7, of which 4 were waited for; matrix products, arithmetic and copies ran while one was open for 11% of the time, Pallas kernels for 0%

commit v1 on v0

--- a/solution.py
+++ b/solution.py
@@ -7,6 +7,11 @@
 NLON = 768
 GROUPS = 4
 GROUP_WIDTH = 32
+
+
+def by_each_axis(array, one, other):
+    half = lax.psum(array, one)
+    return lax.psum(half, other)
 
 
 def build_tables(wave_ids):
@@ -106,7 +111,7 @@
     real_grad = outer_sums[:, :, 0, :, 0, :] + outer_sums[:, :, 1, :, 1, :]
     imag_grad = outer_sums[:, :, 0, :, 1, :] - outer_sums[:, :, 1, :, 0, :]
     local_grad = jnp.stack([real_grad, imag_grad], axis=1).reshape(weights.shape)
-    weight_grad = lax.psum(local_grad.astype(jnp.bfloat16), ("lon", "dp")).astype(jnp.float32)
+    weight_grad = by_each_axis(local_grad.astype(jnp.bfloat16), "dp", "lon").astype(jnp.float32)
     demixed = jnp.einsum(
         "slmqgo,lgpiqo->slmpgi", back_six, kernel, preferred_element_type=jnp.float32
     ).astype(jnp.bfloat16)

time: 735 us -> 558 us (0.76)
  waiting for transfers between devices: 325 us -> 157 us
    psum x1 -> x2, waiting for transfers between devices: 290 us -> 122 us  [the longest x1 66.9 us: by_each_axis(): return lax.psum(half, other)]
  transfers between devices with their start and end apart: 7 -> 8, of which waited for: 4 -> 5; matrix products, arithmetic and copies ran while one was open for 11% -> 13% of each run, Pallas kernels for 0% -> 0%
where the time goes in v1:
time: 558 us; the launch traced here: 548 us
  waiting for transfers between devices  157 us (28%)
  local copies, waits for them, and re-layouts  156 us (28%)
  blocking collectives  131 us (23%)
  matrix products  42.4 us (8%)
  starting transfers between devices  31.2 us (6%)
  other arithmetic  16.4 us (3%)
  between operations  14.6 us (3%)
    psum x1, waiting for transfers between devices, by_each_axis(): return lax.psum(half, other)  66.9 us
    another operation x11, local copies, waits for them, and re-layouts  55.6 us
    psum x1, waiting for transfers between devices, by_each_axis(): half = lax.psum(array, one)  55 us
    all_to_all x2, blocking collectives, analyze(): lax.all_to_all(spectra, 'lon', split_axis=2, concat_axis=1, tiled=True)  50.1 us
    all_to_all x2, blocking collectives, synthesize(): lax.all_to_all(spectral, 'lat', split_axis=2, concat_axis=1, tiled=True)  39.1 us
    another operation x2, local copies, waits for them, and re-layouts, build_kernel(): return jnp.stack([upper_rows, lower_rows], axis=2)  24.2 us
    all_to_all x1, blocking collectives, synthesize(): lax.all_to_all(spectra, 'lat', split_axis=1, concat_axis=2, tiled=True)  21.5 us
    all_to_all x1, blocking collectives, analyze(): lax.all_to_all(lax.all_to_all(spectra, 'lon', split_axis=2, concat_axis=1...  20.1 us
  transfers between devices with their start and end apart: 8, of which 5 were waited for; matrix products, arithmetic and copies ran while one was open for 13% of the time, Pallas kernels for 0%

profile of v1, /device:TPU:8, one launch (start us, length us, event | category | flops | bytes accessed | tf_op | source)
XLA Modules:
  0.0 548.2 jit_solution(1825001330478332372)
XLA Ops:
  8.2 4.9 cosine_multiply_fusion
  13.3 2.2 copy.215
  15.6 3.7 reshape.366
  19.3 2.4 fusion.14
  22.5 25.9 %all_to_all.192 = bf16[1,6,768,128]{3,1,0,2:T(8,128)(2,1)S(1)} all-to-all(bf16[1,6,768,128]{3,1,0,2:T(8,128)(2,1)S(1)} %copy.223), channel_id=1, replica_groups=mesh['lat'=8,'lon'=8,'dp'=4] {'lon'}, dimensions={2} | all-to-all | bytes 2359296 | tf_op jit(solution)/shard_map/all_to_all | solution.py:67
  48.7 1.5 copy.226
  50.1 6.5 %all-to-all-start.1 = ((bf16[1,48,96,128]{3,1,0,2:T(8,128)(2,1)}), bf16[1,48,96,128]{3,1,0,2:T(8,128)(2,1)S(1)}, u32[]{:S(2)}, u32[]{:S(2)}) async-start(bf16[1,48,96,128]{3,1,0,2:T(8,128)(2,1)} %copy.226), calls=%async_computation.1 | async-start | bytes 2359296 | tf_op jit(solution)/shard_map/all_to_all | solution.py:66
  57.4 13.8 %all-to-all-done.1 = bf16[1,48,96,128]{3,1,0,2:T(8,128)(2,1)S(1)} async-done(((bf16[1,48,96,128]{3,1,0,2:T(8,128)(2,1)}), bf16[1,48,96,128]{3,1,0,2:T(8,128)(2,1)S(1)}, u32[]{:S(2)}, u32[]{:S(2)}) %all-to-all-start.1) | async-done | bytes 1179680 | tf_op jit(solution)/shard_map/all_to_all | solution.py:66
  71.2 3.0 copy.280
  74.2 4.4 reshape.378
  78.7 3.4 convolution_convert_fusion.1
  82.1 2.9 copy.229
  85.0 6.4 %all-to-all-start.2 = ((bf16[1,384,12,128]{3,2,0,1:T(8,128)(2,1)}), bf16[1,384,12,128]{3,2,0,1:T(8,128)(2,1)}, u32[]{:S(2)}, u32[]{:S(2)}) async-start(bf16[1,384,12,128]{3,2,0,1:T(8,128)(2,1)} %copy.229), calls=%async_computation.2 | async-start | bytes 3145728 | tf_op jit(solution)/shard_map/all_to_all | solution.py:78
  92.5 1.6 copy.298
  95.3 2.2 copy.299
  97.5 2.7 maximum_bitcast_fusion
  100.2 3.0 pad_maximum_fusion
  103.2 12.7 %copy.232 = bf16[48,4,2,32,2,32]{3,5,2,4,1,0:T(8,128)(2,1)} copy(bf16[48,4,2,32,2,32]{0,5,4,3,1,2:T(8,128)(2,1)} %pad_maximum_fusion) | data formatting | bytes 3145728 | tf_op jit(solution)/shard_map/stack | solution.py:35
  115.8 1.7 copy.230
  117.6 2.7 copy.231
  120.3 8.3 %copy.270 = bf16[48,48,2,4,32,1]{1,4,2,5,3,0:T(8,128)(2,1)} copy(bf16[48,48,2,4,32,1]{0,4,3,2,1,5:T(8,128)(2,1)} %bitcast.179) | data formatting | bytes 2359296 | tf_op jit(solution)/shard_map/reshape.8
  128.5 6.7 %fusion = bf16[1,48,48,2,4,32]{2,5,3,4,1,0:T(8,128)(2,1)} fusion(bf16[48,4,2,32,2,32]{3,5,2,4,1,0:T(8,128)(2,1)} %copy.232, bf16[48,48,2,4,32,1]{1,4,2,5,3,0:T(8,128)(2,1)} %copy.270), kind=kOutput, calls=%fused_computation.4 | convolution fusion | flops 76087296 | bytes 3932160 | tf_op jit(solution)/shard_map/slmpgi,lgpiqo->slmqgo/dot_general | solution.py:101
  135.3 8.3 %copy.234 = bf16[1,48,48,2,4,32]{1,5,4,3,2,0:T(8,128)(2,1)} copy(bf16[1,48,48,2,4,32]{2,5,3,4,1,0:T(8,128)(2,1)} %fusion) | data formatting | bytes 2359296 | tf_op jit(solution)/shard_map/convert_element_type | solution.py:103
  143.5 3.2 copy.235
  146.7 19.4 %all_to_all.193 = bf16[1,48,96,128]{3,1,0,2:T(8,128)(2,1)} all-to-all(bf16[1,48,96,128]{3,1,0,2:T(8,128)(2,1)S(1)} %copy.235), channel_id=1, replica_groups=mesh['lat'=8,'lon'=8,'dp'=4] {'lat'}, dimensions={2} | all-to-all | bytes 2359296 | tf_op jit(solution)/shard_map/all_to_all | solution.py:81
  166.2 4.2 copy.283
  170.4 4.4 reshape.379
  174.8 3.5 convolution_convert_fusion.3
  178.3 2.9 copy.238
  181.2 21.5 %all_to_all.194 = bf16[1,384,12,128]{3,2,0,1:T(8,128)(2,1)S(1)} all-to-all(bf16[1,384,12,128]{3,2,0,1:T(8,128)(2,1)} %copy.238), channel_id=1, replica_groups=mesh['lat'=8,'lon'=8,'dp'=4] {'lat'}, dimensions={1} | all-to-all | bytes 2359296 | tf_op jit(solution)/shard_map/all_to_all | solution.py:88
  204.4 4.3 all-to-all-start.5
  211.1 14.9 %all-to-all-done.5 = bf16[1,48,96,128]{3,2,0,1:T(8,128)(2,1)} async-done(((bf16[1,48,96,128]{3,2,0,1:T(8,128)(2,1)}), bf16[1,48,96,128]{3,2,0,1:T(8,128)(2,1)}, u32[]{:S(2)}, u32[]{:S(2)}) %all-to-all-start.5) | async-done | bytes 1179680 | tf_op jit(solution)/shard_map/all_to_all | solution.py:87
  227.4 4.8 fusion.15
  232.3 2.1 copy.244
  234.4 24.2 %all_to_all.195 = bf16[1,6,768,128]{3,1,0,2:T(8,128)(2,1)S(1)} all-to-all(bf16[1,6,768,128]{3,1,0,2:T(8,128)(2,1)S(1)} %copy.244), channel_id=1, replica_groups=mesh['lat'=8,'lon'=8,'dp'=4] {'lon'}, dimensions={2} | all-to-all | bytes 2359296 | tf_op jit(solution)/shard_map/all_to_all | solution.py:67
  259.3 20.1 %all_to_all.196 = bf16[1,48,96,128]{3,1,0,2:T(8,128)(2,1)S(1)} all-to-all(bf16[1,48,96,128]{3,1,0,2:T(8,128)(2,1)S(1)} %copy.247), channel_id=1, replica_groups=mesh['lat'=8,'lon'=8,'dp'=4] {'lat'}, dimensions={2} | all-to-all | bytes 2359296 | tf_op jit(solution)/shard_map/all_to_all | solution.py:66
  279.4 3.0 copy.284
  282.4 4.4 reshape.380
  286.8 2.4 convolution_convert_fusion
  289.2 2.0 copy.250
  291.1 5.1 all-to-all-start.8
  296.3 11.6 %copy.253 = bf16[48,4,2,32,2,32]{5,3,4,2,1,0:T(8,128)(2,1)} copy(bf16[48,4,2,32,2,32]{0,5,4,3,1,2:T(8,128)(2,1)} %pad_maximum_fusion) | data formatting | bytes 3145728 | tf_op jit(solution)/shard_map/stack | solution.py:35
  307.8 6.3 %all-to-all-done.8 = bf16[1,384,12,128]{3,2,0,1:T(8,128)(2,1)S(1)} async-done(((bf16[1,384,12,128]{3,2,0,1:T(8,128)(2,1)}), bf16[1,384,12,128]{3,2,0,1:T(8,128)(2,1)S(1)}, u32[]{:S(2)}, u32[]{:S(2)}) %all-to-all-start.8) | async-done | bytes 1179680 | tf_op jit(solution)/shard_map/all_to_all | solution.py:78
  314.5 2.7 copy.252
  317.2 8.2 %copy.273 = bf16[48,48,2,4,32,1]{1,4,2,5,3,0:T(8,128)(2,1)} copy(bf16[48,48,2,4,32,1]{0,4,3,2,1,5:T(8,128)(2,1)} %bitcast.182) | data formatting | bytes 2359296 | tf_op jit(solution)/shard_map/reshape.39
  325.5 6.7 %fusion.1 = bf16[1,48,48,2,4,32]{2,5,3,4,1,0:T(8,128)(2,1)} fusion(bf16[48,4,2,32,2,32]{5,3,4,2,1,0:T(8,128)(2,1)} %copy.253, bf16[48,48,2,4,32,1]{1,4,2,5,3,0:T(8,128)(2,1)} %copy.273), kind=kOutput, calls=%fused_computation.5 | convolution fusion | flops 76087296 | bytes 3932160 | tf_op jit(solution)/shard_map/slmqgo,lgpiqo->slmpgi/dot_general | solution.py:115
  332.2 8.3 %copy.255 = bf16[1,48,48,2,4,32]{1,5,4,3,2,0:T(8,128)(2,1)} copy(bf16[1,48,48,2,4,32]{2,5,3,4,1,0:T(8,128)(2,1)} %fusion.1) | data formatting | bytes 2359296 | tf_op jit(solution)/shard_map/convert_element_type | solution.py:117
  340.4 3.2 copy.256
  343.6 19.7 %all_to_all.197 = bf16[1,48,96,128]{3,1,0,2:T(8,128)(2,1)S(1)} all-to-all(bf16[1,48,96,128]{3,1,0,2:T(8,128)(2,1)S(1)} %copy.256), channel_id=1, replica_groups=mesh['lat'=8,'lon'=8,'dp'=4] {'lat'}, dimensions={2} | all-to-all | bytes 2359296 | tf_op jit(solution)/shard_map/all_to_all | solution.py:81
  363.3 3.0 copy.287
  366.3 4.4 reshape.381
  370.7 2.4 convolution_convert_fusion.2
  373.2 2.0 copy.259
  375.2 5.1 all-to-all-start.10
  380.5 8.3 %copy.276 = bf16[48,48,2,4,32,1]{1,4,5,2,3,0:T(8,128)(2,1)} copy(bf16[48,48,2,4,32,1]{0,4,3,2,1,5:T(8,128)(2,1)} %bitcast.180) | data formatting | bytes 2359296 | tf_op jit(solution)/shard_map/reshape.8
  388.7 8.0 %fusion.41 = f32[48,4,2,32,2,32]{5,3,4,2,1,0:T(8,128)S(1)} fusion(bf16[48,48,2,4,32,1]{1,4,5,2,3,0:T(8,128)(2,1)} %copy.276, bf16[48,48,2,4,32,1]{1,4,2,5,3,0:T(8,128)(2,1)} %copy.273), kind=kOutput, calls=%fused_computation.66 | convolution fusion | flops 75497472 | bytes 5505024 | tf_op jit(solution)/shard_map/slmpgi,slmqgo->lgpiqo/dot_general | solution.py:108
  396.7 3.2 fusion.3
  399.9 2.9 reshape.382
  402.9 2.9 reshape.383
  408.7 3.7 all-to-all-start.11
  412.4 55.0 %all-reduce.3.cloned.1.call-done = bf16[48,2,4,1024]{3,0,2,1:T(8,128)(2,1)} async-done(((bf16[48,2,4,1024]{3,0,2,1:T(8,128)(2,1)}), bf16[48,2,4,1024]{3,0,2,1:T(8,128)(2,1)}) %all-reduce.3.cloned.1.call-update) | async-done | bytes 786448 | tf_op jit(solution)/shard_map/psum | solution.py:13
  467.9 66.9 %all-reduce.5.cloned.1.call-done = bf16[48,2,4,1024]{3,0,2,1:T(8,128)(2,1)} async-done(((bf16[48,2,4,1024]{3,0,2,1:T(8,128)(2,1)}), bf16[48,2,4,1024]{3,0,2,1:T(8,128)(2,1)}) %all-reduce.5.cloned.1.call-update) | async-done | bytes 786448 | tf_op jit(solution)/shard_map/psum | solution.py:14
  534.9 2.9 copy.269
  539.0 2.2 fusion.5
  (49 shorter events, 16.9 us)
Async XLA Ops:
  7.2 12.2 %copy-start = (bf16[1,6,768,128]{3,2,1,0:T(8,128)(2,1)S(1)}, bf16[1,6,768,128]{3,2,1,0:T(8,128)(2,1)}, u32[]{:S(2)}) copy-start(bf16[1,6,768,128]{3,2,1,0:T(8,128)(2,1)} %param.5) | copy-start | bytes 3538948
  50.1 21.1 %all-to-all-start.1 = ((bf16[1,48,96,128]{3,1,0,2:T(8,128)(2,1)}), bf16[1,48,96,128]{3,1,0,2:T(8,128)(2,1)S(1)}, u32[]{:S(2)}, u32[]{:S(2)}) async-start(bf16[1,48,96,128]{3,1,0,2:T(8,128)(2,1)} %copy.226), calls=%async_computation.1 | async-start | bytes 2359296 | tf_op jit(solution)/shard_map/all_to_all | solution.py:66
  85.0 6.4 %copy-start.3 = (bf16[48,2,4,1024]{3,2,1,0:T(4,128)(2,1)S(1)}, bf16[48,2,4,1024]{3,2,1,0:T(4,128)(2,1)}, u32[]{:S(2)}) copy-start(bf16[48,2,4,1024]{3,2,1,0:T(4,128)(2,1)} %param.9) | copy-start | bytes 2359300
  85.0 30.9 %all-to-all-start.2 = ((bf16[1,384,12,128]{3,2,0,1:T(8,128)(2,1)}), bf16[1,384,12,128]{3,2,0,1:T(8,128)(2,1)}, u32[]{:S(2)}, u32[]{:S(2)}) async-start(bf16[1,384,12,128]{3,2,0,1:T(8,128)(2,1)} %copy.229), calls=%async_computation.2 | async-start | bytes 3145728 | tf_op jit(solution)/shard_map/all_to_all | solution.py:78
  204.4 21.6 %all-to-all-start.5 = ((bf16[1,48,96,128]{3,2,0,1:T(8,128)(2,1)}), bf16[1,48,96,128]{3,2,0,1:T(8,128)(2,1)}, u32[]{:S(2)}, u32[]{:S(2)}) async-start(bf16[1,48,96,128]{3,2,0,1:T(8,128)(2,1)} %copy.241), calls=%async_computation.5 | async-start | bytes 2359296 | tf_op jit(solution)/shard_map/all_to_all | solution.py:87
  291.1 23.0 %all-to-all-start.8 = ((bf16[1,384,12,128]{3,2,0,1:T(8,128)(2,1)}), bf16[1,384,12,128]{3,2,0,1:T(8,128)(2,1)S(1)}, u32[]{:S(2)}, u32[]{:S(2)}) async-start(bf16[1,384,12,128]{3,2,0,1:T(8,128)(2,1)} %copy.250), calls=%async_computation.8 | async-start | bytes 3145728 | tf_op jit(solution)/shard_map/all_to_all | solution.py:78
  375.2 31.8 %all-to-all-start.10 = ((bf16[1,384,12,128]{3,2,0,1:T(8,128)(2,1)}), bf16[1,384,12,128]{3,2,0,1:T(8,128)(2,1)S(1)}, u32[]{:S(2)}, u32[]{:S(2)}) async-start(bf16[1,384,12,128]{3,2,0,1:T(8,128)(2,1)} %copy.259), calls=%async_computation.10 | async-start | bytes 3145728 | tf_op jit(solution)/shard_map/all_to_all | solution.py:88
  380.3 87.1 %all-reduce.3.cloned.1.call-start = ((), (), s32[]{:S(2)}) async-start(), calls=%async_computation.12 | async-start | bytes 1572864 | tf_op jit(solution)/shard_map/psum | solution.py:13
  408.7 58.7 %copy-start.2 = (bf16[384,2,768]{2,1,0:T(2,128)(2,1)S(1)}, bf16[384,2,768]{2,1,0:T(2,128)(2,1)}, u32[]{:S(2)}) copy-start(bf16[384,2,768]{2,1,0:T(2,128)(2,1)} %copy.215) | copy-start | bytes 3538948
  408.7 129.1 %all-to-all-start.11 = ((bf16[1,48,96,128]{3,2,0,1:T(8,128)(2,1)}), bf16[1,48,96,128]{3,2,0,1:T(8,128)(2,1)S(1)}, u32[]{:S(2)}, u32[]{:S(2)}) async-start(bf16[1,48,96,128]{3,2,0,1:T(8,128)(2,1)} %copy.262), calls=%async_computation.11 | async-start | bytes 2359296 | tf_op jit(solution)/shard_map/all_to_all | solution.py:87
  412.4 122.5 %all-reduce.5.cloned.1.call-start = ((), (), s32[]{:S(2)}) async-start(), calls=%async_computation.13 | async-start | bytes 1572864 | tf_op jit(solution)/shard_map/psum | solution.py:14
  537.7 1.3 copy-start.4
  539.0 2.2 copy-start.1
Sparse Core Ops, SparseCore 0:
  407.0 60.3 all-reduce.2
  469.8 65.0 all-reduce.4
